TPU v7x, 32 devices: a whole 2x2x4 slice. The times are simulated.
32 devices in a mesh: ri: 4 (over z), ao: 8 (over y, x, core).
Axes of the slice: x: 2, y: 2, z: 4, core: 2. Of those that a mesh axis runs over, the one named last changes fastest.
Arguments:
- tensor: bfloat16 [512, 256, 256], P('ri', 'ao'), may hold values from -0.5 to 0.5
- live_blocks: int32 [8, 8, 8], P('ri', 'ao'), may hold values 0 or 1
- occ_density: bfloat16 [256, 256], P('ao'), may hold values from -0.375 to 0.375
- virt_density: bfloat16 [256, 256], P('ao'), may hold values from -0.375 to 0.375
- occ_mask: int32 [8, 8], P('ao'), may hold values 0 or 1
- virt_mask: int32 [8, 8], P('ao'), may hold values 0 or 1
- pair_slots: int32 [8, 8], P('ao'), may hold values from 0 to 7, as said below
Outputs:
- polar: float32 [512, 512], P('ri', 'ao')
Inputs may be any that keep to these rules, and one draw needn't show every extreme that they name: pair_slots[b, 0] = b, and the 8 entries of a row are different AO blocks.
All inputs are finite; a program needn't handle non-finite values. No bound on the sum of `live_blocks` or of `occ_mask` or of `virt_mask` on one device may be relied on, other than what follows from the above.
Results may differ from a plain program's by a relative error of at most 0.0041.
Values may be sent and summed in bfloat16 or wider, within the bound.
No kernel may reach another device: no remote copies, remote signals or barrier semaphores. Data moves between devices by JAX's collectives and lax.ppermute only.
A program may use at most 192 MiB of HBM per device.

v0:
```python
import jax
import jax.numpy as jnp
from jax import lax
from jax.sharding import PartitionSpec as P

BS = 32
KS = 8
RB = 64


def shifted(block, axis, distance):
    devices = range(lax.axis_size(axis))
    route = [((i - distance) % len(devices), i) for i in devices]
    return lax.ppermute(block, axis, route)


def screen_density(density, block_mask):
    own_blocks = block_mask.shape[0]
    all_blocks = block_mask.shape[1]
    shaped = density.reshape(own_blocks, BS, all_blocks, BS)
    keeper = block_mask.astype(density.dtype)[:, None, :, None]
    return (shaped * keeper).reshape(density.shape)


def pick_slots(pair_slots, stacked, first_block):
    own_blocks = stacked.shape[1] // BS
    block_ids = first_block + jnp.arange(own_blocks, dtype=jnp.int32)
    matches = (pair_slots[:, :, None] == block_ids[None, None, :]).astype(jnp.bfloat16)
    shaped = stacked.reshape(2, own_blocks, BS, stacked.shape[2])
    return jnp.einsum("bkc,tcjn->tbkjn", matches, shaped, preferred_element_type=jnp.float32)


def per_device(tensor, live_blocks, occ_density, virt_density, occ_mask, virt_mask, pair_slots):
    own_rows = tensor.shape[0]
    own_width = tensor.shape[1]
    own_blocks = own_width // BS
    groups = live_blocks.shape[0]
    keeper = live_blocks.astype(jnp.bfloat16)[:, None, :, None, :, None]
    tensor_eff = (tensor.reshape(groups, RB, own_blocks, BS, KS, BS) * keeper).reshape(tensor.shape)
    stacked = jnp.stack(
        [screen_density(occ_density, occ_mask), screen_density(virt_density, virt_mask)]
    )
    ao_total = stacked.shape[2]
    cycle_size = lax.axis_size("ao")
    position = lax.axis_index("ao")

    def visit(turn_index, state):
        current, gathered_rows = state
        current = shifted(current, "ao", 1)
        source = (position - turn_index + cycle_size) % cycle_size
        return (current, gathered_rows + pick_slots(pair_slots, current, source * own_blocks))

    start_pick = pick_slots(pair_slots, stacked, position * own_blocks)
    unused, picked = lax.fori_loop(1, cycle_size, visit, (stacked, start_pick))
    picked = picked.astype(jnp.bfloat16)
    occ_rows = picked[0]
    virt_rows = picked[1]
    span_cols = min(128, ao_total)
    piece_count = ao_total // span_cols
    tensor_five = tensor_eff.reshape(own_rows, own_blocks, BS, KS, BS)
    occ_pieces = occ_rows.reshape(own_blocks, KS, BS, piece_count, span_cols)

    def occ_piece(piece_index):
        columns = lax.dynamic_index_in_dim(occ_pieces, piece_index, 3, keepdims=False)
        product = jnp.einsum(
            "pbikj,bkjl->lbip", tensor_five, columns, preferred_element_type=jnp.float32
        )
        return product.astype(jnp.bfloat16).reshape(span_cols, own_width, own_rows)

    half_occ = lax.map(occ_piece, jnp.arange(piece_count, dtype=jnp.int32)).reshape(
        ao_total, own_width, own_rows
    )
    half_occ_local = lax.all_to_all(half_occ, "ao", split_axis=0, concat_axis=1, tiled=True)

    def virt_piece(source_rows, piece_index):
        columns = lax.dynamic_slice_in_dim(virt_rows, piece_index * span_cols, span_cols, 3)
        product = jnp.einsum(
            "qbikj,bkjn->qbin", source_rows, columns, preferred_element_type=jnp.float32
        )
        return product.astype(jnp.bfloat16).reshape(source_rows.shape[0], own_width, span_cols)

    all_tensor = lax.all_gather(tensor_eff, "ri", axis=0, tiled=True)
    kept_rows = all_tensor.shape[0] // cycle_size
    source_rows = all_tensor
    polar_source_rows = source_rows.reshape(kept_rows * lax.axis_size("ao"), own_blocks, BS, KS, BS)

    def add_piece(piece_index, running):
        virt_part = virt_piece(polar_source_rows, piece_index)
        occ_part = lax.dynamic_slice_in_dim(half_occ_local, piece_index * span_cols, span_cols, 1)
        return running + jnp.einsum(
            "qln,lnp->qp", virt_part, occ_part, preferred_element_type=jnp.float32
        )

    polar_block = lax.psum_scatter(
        lax.fori_loop(
            0,
            piece_count,
            add_piece,
            jnp.zeros((polar_source_rows.shape[0], own_rows), jnp.float32),
        ),
        "ao",
        scatter_dimension=0,
        tiled=True,
    )
    return polar_block.T


def solution(mesh):
    placed = (
        P("ri", "ao", None),
        P("ri", "ao", None),
        P("ao", None),
        P("ao", None),
        P("ao", None),
        P("ao", None),
        P("ao", None),
    )
    return jax.shard_map(
        per_device, mesh=mesh, in_specs=placed, out_specs=P("ri", "ao"), check_vma=False
    )
```

profile of v0, /device:TPU:0, one launch (start us, length us, event | category | flops | bytes accessed | tf_op | source)
XLA Modules:
  0.0 228.5 jit_solution(457382478721264577)
XLA Ops:
  6.5 0.7 convert_element_type.41
  7.2 0.1 copy.51
  7.3 0.1 mul.93
  7.5 0.1 mul.94
  7.6 0.1 copy.41
  7.7 3.1 %broadcast_multiply_fusion.1 = bf16[128,32,256]{2,1,0:T(8,128)(2,1)} fusion(bf16[128,32,256]{2,1,0:T(8,128)(2,1)} %param.13, bf16[128,256]{1,0:T(8,128)(2,1)S(1)} %copy.41), kind=kLoop, calls=%fused_computation.23 | loop fusion | flops 1048576 | bytes 4259840 | tf_op jit(solution)/shard_map/mul | solution.py:39
  10.8 0.0 all-gather.2.cloned.1.call-update
  10.9 1.6 copy-done.1
  12.4 0.0 copy-start.9
  12.5 3.1 %copy.43 = bf16[128,32,256]{0,2,1:T(8,128)(2,1)} copy(bf16[128,32,256]{2,1,0:T(8,128)(2,1)S(1)} %copy-done.1) | data formatting | bytes 4194304 | tf_op args[0]
  15.6 0.1 mul.87
  15.6 0.1 mul.88
  15.7 0.1 mul.81
  15.8 0.1 mul.82
  16.0 0.1 multiply_bitcast_fusion
  16.1 32.0 %while.41 = (s32[]{:T(128)}, bf16[2,32,256]{2,1,0:T(8,128)(2,1)S(1)}, f32[2,1,8,32,256]{4,3,2,1,0:T(8,128)S(1)}, s32[]{:T(128)}, s32[1,8]{1,0:T(1,128)S(1)}, /*index=5*/s32[]{:T(128)}, s32[]{:T(128)}, s32[]{:T(128)}, s32[]{:T(128)}) while((s32[]{:T(128)}, bf16[2,32,256]{2,1,0:T(8,128)(2,1)S(1)}, f32[2,1,8,32,256]{4,3,2,1,0:T(8,128)S(1)}, ...), condition=%wide.region_1.2_spmd, body=%wide.region_0.1_spmd.sunk | while | flops 278559 | bytes 1409390 | solution.py:54
  16.1 0.5 collective-permute-start
  16.6 4.5 %collective-permute-done = bf16[2,32,256]{2,1,0:T(8,128)(2,1)S(1)} collective-permute-done((bf16[2,32,256]{2,1,0:T(8,128)(2,1)S(1)}, bf16[2,32,256]{2,1,0:T(8,128)(2,1)S(1)}, u32[]{:S(2)}, u32[]{:S(2)}) %collective-permute-start) | collective-permute-done | bytes 32800 | tf_op jit(solution)/shard_map/while/body/eval_jaxpr/ppermute | solution.py:14
  21.1 0.1 bitcast_add_fusion.2
  21.2 0.1 collective-permute-start
  21.3 4.2 %collective-permute-done = bf16[2,32,256]{2,1,0:T(8,128)(2,1)S(1)} collective-permute-done((bf16[2,32,256]{2,1,0:T(8,128)(2,1)S(1)}, bf16[2,32,256]{2,1,0:T(8,128)(2,1)S(1)}, u32[]{:S(2)}, u32[]{:S(2)}) %collective-permute-start) | collective-permute-done | bytes 32800 | tf_op jit(solution)/shard_map/while/body/eval_jaxpr/ppermute | solution.py:14
  25.5 0.1 bitcast_add_fusion.2
  25.7 0.1 collective-permute-start
  25.8 4.2 %collective-permute-done = bf16[2,32,256]{2,1,0:T(8,128)(2,1)S(1)} collective-permute-done((bf16[2,32,256]{2,1,0:T(8,128)(2,1)S(1)}, bf16[2,32,256]{2,1,0:T(8,128)(2,1)S(1)}, u32[]{:S(2)}, u32[]{:S(2)}) %collective-permute-start) | collective-permute-done | bytes 32800 | tf_op jit(solution)/shard_map/while/body/eval_jaxpr/ppermute | solution.py:14
  30.0 0.1 bitcast_add_fusion.2
  30.2 0.1 collective-permute-start
  30.3 4.2 %collective-permute-done = bf16[2,32,256]{2,1,0:T(8,128)(2,1)S(1)} collective-permute-done((bf16[2,32,256]{2,1,0:T(8,128)(2,1)S(1)}, bf16[2,32,256]{2,1,0:T(8,128)(2,1)S(1)}, u32[]{:S(2)}, u32[]{:S(2)}) %collective-permute-start) | collective-permute-done | bytes 32800 | tf_op jit(solution)/shard_map/while/body/eval_jaxpr/ppermute | solution.py:14
  34.5 0.1 bitcast_add_fusion.2
  34.7 0.1 collective-permute-start
  34.8 4.2 %collective-permute-done = bf16[2,32,256]{2,1,0:T(8,128)(2,1)S(1)} collective-permute-done((bf16[2,32,256]{2,1,0:T(8,128)(2,1)S(1)}, bf16[2,32,256]{2,1,0:T(8,128)(2,1)S(1)}, u32[]{:S(2)}, u32[]{:S(2)}) %collective-permute-start) | collective-permute-done | bytes 32800 | tf_op jit(solution)/shard_map/while/body/eval_jaxpr/ppermute | solution.py:14
  39.0 0.1 bitcast_add_fusion.2
  39.1 0.1 collective-permute-start
  39.2 4.2 %collective-permute-done = bf16[2,32,256]{2,1,0:T(8,128)(2,1)S(1)} collective-permute-done((bf16[2,32,256]{2,1,0:T(8,128)(2,1)S(1)}, bf16[2,32,256]{2,1,0:T(8,128)(2,1)S(1)}, u32[]{:S(2)}, u32[]{:S(2)}) %collective-permute-start) | collective-permute-done | bytes 32800 | tf_op jit(solution)/shard_map/while/body/eval_jaxpr/ppermute | solution.py:14
  43.4 0.1 bitcast_add_fusion.2
  43.6 0.1 collective-permute-start
  43.7 4.2 %collective-permute-done = bf16[2,32,256]{2,1,0:T(8,128)(2,1)S(1)} collective-permute-done((bf16[2,32,256]{2,1,0:T(8,128)(2,1)S(1)}, bf16[2,32,256]{2,1,0:T(8,128)(2,1)S(1)}, u32[]{:S(2)}, u32[]{:S(2)}) %collective-permute-start) | collective-permute-done | bytes 32800 | tf_op jit(solution)/shard_map/while/body/eval_jaxpr/ppermute | solution.py:14
  47.9 0.1 bitcast_add_fusion.2
  48.2 0.1 mul.97
  48.3 0.1 mul.98
  48.3 1.7 broadcast_multiply_fusion
  50.1 12.4 %while.42 = (s32[]{:T(128)}, bf16[2,128,32,128]{3,2,1,0:T(8,128)(2,1)}, s32[2]{0:T(128)S(1)}, bf16[1,8,32,2,128]{4,2,1,3,0:T(8,128)(2,1)S(1)}, bf16[128,1,32,8,3...) while((s32[]{:T(128)}, bf16[2,128,32,128]{3,2,1,0:T(8,128)(2,1)}, s32[2]{0:T(128)S(1)}, ...), condition=%wide.region_3.4_spmd, body=%wide.region_2.3_spmd.sunk | while | flops 268959744 | bytes 22085836 | solution.py:70
  50.1 0.6 dynamic_slice.40
  52.7 0.5 fusion.52
  53.1 1.1 copy-done.3
  54.3 0.7 copy_dynamic-update-slice_fusion.2
  55.0 1.3 copy-done.4
  56.3 0.6 dynamic_slice.40
  58.9 0.5 fusion.52
  59.3 1.1 copy-done.3
  60.4 0.7 copy_dynamic-update-slice_fusion.2
  61.2 1.3 copy-done.4
  62.5 3.6 %all-to-all-start = ((bf16[256,32,128]{2,1,0:T(8,128)(2,1)}), bf16[256,32,128]{2,1,0:T(8,128)(2,1)S(1)}, u32[]{:S(2)}, u32[]{:S(2)}) async-start(bf16[256,32,128]{2,1,0:T(8,128)(2,1)} %bitcast.132), calls=%async_computation | async-start | bytes 4194304 | tf_op jit(solution)/shard_map/all_to_all | solution.py:73
  66.1 0.0 reduce-scatter.2.cloned.1.call-start
  66.2 26.5 %all-to-all-done = bf16[256,32,128]{2,1,0:T(8,128)(2,1)S(1)} async-done(((bf16[256,32,128]{2,1,0:T(8,128)(2,1)}), bf16[256,32,128]{2,1,0:T(8,128)(2,1)S(1)}, u32[]{:S(2)}, u32[]{:S(2)}) %all-to-all-start) | async-done | bytes 2097184 | tf_op jit(solution)/shard_map/all_to_all | solution.py:73
  92.7 1.3 copy-done.2
  94.0 2.2 copy.47
  96.3 67.1 %all-gather.2.cloned.1.call-done = bf16[512,32,256]{2,1,0:T(8,128)(2,1)} async-done(((bf16[128,32,256]{2,1,0:T(8,128)(2,1)}), bf16[512,32,256]{2,1,0:T(8,128)(2,1)}) %all-gather.2.cloned.1.call-update) | async-done | bytes 8388624 | tf_op jit(solution)/shard_map/all_gather | solution.py:82
  163.4 13.8 %copy.42 = bf16[512,32,256]{0,2,1:T(8,128)(2,1)} copy(bf16[512,32,256]{2,1,0:T(8,128)(2,1)} %all-gather.2.cloned.1.call-done) | data formatting | bytes 16777216 | tf_op jit(solution)/shard_map/all_gather | solution.py:82
  177.2 11.8 %while.43 = (s32[]{:T(128)}, f32[512,128]{1,0:T(8,128)S(1)}, bf16[1,8,32,256]{3,2,1,0:T(8,128)(2,1)S(1)}, bf16[512,1,32,8,32]{0,4,3,2,1:T(8,128)(2,1)}, bf16[32,...) while((s32[]{:T(128)}, f32[512,128]{1,0:T(8,128)S(1)}, ...), condition=%wide.region_5.6_spmd.clone, body=%wide.region_4.5_spmd.clone.sunk | while | flops 1612840960 | bytes 10028700 | solution.py:95
  177.2 5.9 %fusion.57 = f32[512,128]{1,0:T(8,128)S(1)} fusion(bf16[512,1,32,8,32]{0,4,3,2,1:T(8,128)(2,1)} %get-tuple-element.511, bf16[32,256,128]{2,1,0:T(8,128)(2,1)S(1)} %get-tuple-element.512, s32[]{:T(128)S(6)} %select_n.38, f32[512,128]{1,0:T(8,128)S(1)} %get-tuple-element.500, pred[]{:T(512)S(6)} %compare.4, ...), kind=kOutput, calls=%fused_computation.17.clone.1 | convolution fusion | flops 1612840960 | bytes 10028544 | tf_op jit(solution)/shard_map/while/body/eval_jaxpr/qln,lnp->qp/dot_general | solution.py:90
  183.1 5.9 %fusion.57 = f32[512,128]{1,0:T(8,128)S(1)} fusion(bf16[512,1,32,8,32]{0,4,3,2,1:T(8,128)(2,1)} %get-tuple-element.511, bf16[32,256,128]{2,1,0:T(8,128)(2,1)S(1)} %get-tuple-element.512, s32[]{:T(128)S(6)} %select_n.38, f32[512,128]{1,0:T(8,128)S(1)} %get-tuple-element.500, pred[]{:T(512)S(6)} %compare.4, ...), kind=kOutput, calls=%fused_computation.17.clone.1 | convolution fusion | flops 1612840960 | bytes 10028544 | tf_op jit(solution)/shard_map/while/body/eval_jaxpr/qln,lnp->qp/dot_general | solution.py:90
  189.0 0.7 copy-done
  189.7 0.0 reduce-scatter.2.cloned.1.call-update
  189.7 32.0 %reduce-scatter.2.cloned.1.call-done = f32[64,128]{1,0:T(8,128)} async-done(((f32[512,128]{1,0:T(8,128)}), f32[64,128]{1,0:T(8,128)}) %reduce-scatter.2.cloned.1.call-update) | async-done | bytes 32784 | tf_op jit(solution)/shard_map/reduce_scatter | solution.py:94
  (50 shorter events, 0.3 us)
Async XLA Ops:
  6.5 156.8 %all-gather.2.cloned.1.call-start = ((), (), s32[]{:S(2)}) async-start(), calls=%async_computation.2 | async-start | bytes 10485760 | tf_op jit(solution)/shard_map/all_gather | solution.py:82
  10.8 1.6 copy-start.1
  12.4 3.1 %copy-start.7 = (s32[1,8]{1,0:T(1,128)S(1)}, s32[1,8]{1,0:T(1,128)}, u32[]{:S(2)}) copy-start(s32[1,8]{1,0:T(1,128)} %param.18) | copy-start | bytes 100
  12.4 3.3 %copy-start.8 = (s32[1,8]{1,0:T(1,128)S(1)}, s32[1,8]{1,0:T(1,128)}, u32[]{:S(2)}) copy-start(s32[1,8]{1,0:T(1,128)} %param.17) | copy-start | bytes 100
  12.4 3.5 %copy-start.5 = (bf16[32,256]{1,0:T(8,128)(2,1)S(1)}, bf16[32,256]{1,0:T(8,128)(2,1)}, u32[]{:S(2)}) copy-start(bf16[32,256]{1,0:T(8,128)(2,1)} %param.16) | copy-start | bytes 49156
  12.4 3.5 %copy-start.6 = (bf16[32,256]{1,0:T(8,128)(2,1)S(1)}, bf16[32,256]{1,0:T(8,128)(2,1)}, u32[]{:S(2)}) copy-start(bf16[32,256]{1,0:T(8,128)(2,1)} %param.15) | copy-start | bytes 49156
  12.4 3.5 %copy-start.9 = (s32[1,8]{1,0:T(1,128)S(1)}, s32[1,8]{1,0:T(1,128)}, u32[]{:S(2)}) copy-start(s32[1,8]{1,0:T(1,128)} %param.19) | copy-start | bytes 100
  16.1 5.0 %collective-permute-start = (bf16[2,32,256]{2,1,0:T(8,128)(2,1)S(1)}, bf16[2,32,256]{2,1,0:T(8,128)(2,1)S(1)}, u32[]{:S(2)}, u32[]{:S(2)}) collective-permute-start(bf16[2,32,256]{2,1,0:T(8,128)(2,1)S(1)} %get-tuple-element.449), channel_id=1, source_target_pairs={{7,0},{0,1},{1,2},{2,3},{3,4},{4,5},{5,6},{6,7},{15,8},{8,9},{9,10... | collective-permute-start | bytes 98312 | tf_op jit(solution)/shard_map/while/body/eval_jaxpr/ppermute | solution.py:14
  21.2 4.3 %collective-permute-start = (bf16[2,32,256]{2,1,0:T(8,128)(2,1)S(1)}, bf16[2,32,256]{2,1,0:T(8,128)(2,1)S(1)}, u32[]{:S(2)}, u32[]{:S(2)}) collective-permute-start(bf16[2,32,256]{2,1,0:T(8,128)(2,1)S(1)} %get-tuple-element.449), channel_id=1, source_target_pairs={{7,0},{0,1},{1,2},{2,3},{3,4},{4,5},{5,6},{6,7},{15,8},{8,9},{9,10... | collective-permute-start | bytes 98312 | tf_op jit(solution)/shard_map/while/body/eval_jaxpr/ppermute | solution.py:14
  25.7 4.3 %collective-permute-start = (bf16[2,32,256]{2,1,0:T(8,128)(2,1)S(1)}, bf16[2,32,256]{2,1,0:T(8,128)(2,1)S(1)}, u32[]{:S(2)}, u32[]{:S(2)}) collective-permute-start(bf16[2,32,256]{2,1,0:T(8,128)(2,1)S(1)} %get-tuple-element.449), channel_id=1, source_target_pairs={{7,0},{0,1},{1,2},{2,3},{3,4},{4,5},{5,6},{6,7},{15,8},{8,9},{9,10... | collective-permute-start | bytes 98312 | tf_op jit(solution)/shard_map/while/body/eval_jaxpr/ppermute | solution.py:14
  30.2 4.3 %collective-permute-start = (bf16[2,32,256]{2,1,0:T(8,128)(2,1)S(1)}, bf16[2,32,256]{2,1,0:T(8,128)(2,1)S(1)}, u32[]{:S(2)}, u32[]{:S(2)}) collective-permute-start(bf16[2,32,256]{2,1,0:T(8,128)(2,1)S(1)} %get-tuple-element.449), channel_id=1, source_target_pairs={{7,0},{0,1},{1,2},{2,3},{3,4},{4,5},{5,6},{6,7},{15,8},{8,9},{9,10... | collective-permute-start | bytes 98312 | tf_op jit(solution)/shard_map/while/body/eval_jaxpr/ppermute | solution.py:14
  34.7 4.3 %collective-permute-start = (bf16[2,32,256]{2,1,0:T(8,128)(2,1)S(1)}, bf16[2,32,256]{2,1,0:T(8,128)(2,1)S(1)}, u32[]{:S(2)}, u32[]{:S(2)}) collective-permute-start(bf16[2,32,256]{2,1,0:T(8,128)(2,1)S(1)} %get-tuple-element.449), channel_id=1, source_target_pairs={{7,0},{0,1},{1,2},{2,3},{3,4},{4,5},{5,6},{6,7},{15,8},{8,9},{9,10... | collective-permute-start | bytes 98312 | tf_op jit(solution)/shard_map/while/body/eval_jaxpr/ppermute | solution.py:14
  39.1 4.3 %collective-permute-start = (bf16[2,32,256]{2,1,0:T(8,128)(2,1)S(1)}, bf16[2,32,256]{2,1,0:T(8,128)(2,1)S(1)}, u32[]{:S(2)}, u32[]{:S(2)}) collective-permute-start(bf16[2,32,256]{2,1,0:T(8,128)(2,1)S(1)} %get-tuple-element.449), channel_id=1, source_target_pairs={{7,0},{0,1},{1,2},{2,3},{3,4},{4,5},{5,6},{6,7},{15,8},{8,9},{9,10... | collective-permute-start | bytes 98312 | tf_op jit(solution)/shard_map/while/body/eval_jaxpr/ppermute | solution.py:14
  43.6 4.3 %collective-permute-start = (bf16[2,32,256]{2,1,0:T(8,128)(2,1)S(1)}, bf16[2,32,256]{2,1,0:T(8,128)(2,1)S(1)}, u32[]{:S(2)}, u32[]{:S(2)}) collective-permute-start(bf16[2,32,256]{2,1,0:T(8,128)(2,1)S(1)} %get-tuple-element.449), channel_id=1, source_target_pairs={{7,0},{0,1},{1,2},{2,3},{3,4},{4,5},{5,6},{6,7},{15,8},{8,9},{9,10... | collective-permute-start | bytes 98312 | tf_op jit(solution)/shard_map/while/body/eval_jaxpr/ppermute | solution.py:14
  52.6 1.6 copy-start.3
  55.0 1.3 copy-start.4
  58.9 1.6 copy-start.3
  61.2 1.3 copy-start.4
  62.5 30.2 %all-to-all-start = ((bf16[256,32,128]{2,1,0:T(8,128)(2,1)}), bf16[256,32,128]{2,1,0:T(8,128)(2,1)S(1)}, u32[]{:S(2)}, u32[]{:S(2)}) async-start(bf16[256,32,128]{2,1,0:T(8,128)(2,1)} %bitcast.132), calls=%async_computation | async-start | bytes 4194304 | tf_op jit(solution)/shard_map/all_to_all | solution.py:73
  66.1 155.6 %reduce-scatter.2.cloned.1.call-start = ((), (), s32[]{:S(2)}) async-start(), calls=%async_computation.3 | async-start | bytes 294912 | tf_op jit(solution)/shard_map/reduce_scatter | solution.py:94
  92.7 1.3 copy-start.2
  189.0 0.7 copy-start
Sparse Core Ops, SparseCore 0:
  11.0 152.3 all-gather.1
  189.8 31.8 reduce-scatter.1
where the time goes:
time: 229 us
  waiting for transfers between devices  155 us (68%)
  local copies, waits for them, and re-layouts  31.3 us (14%)
  between operations  13.6 us (6%)
  matrix products  12.7 us (6%)
  other arithmetic  6.8 us (3%)
  starting transfers between devices  4.5 us (2%)
  loops' own time  4.39 us (2%)
    all_gather x1, waiting for transfers between devices, per_device(): all_tensor = lax.all_gather(tensor_eff, 'ri', axis=0, tiled=True)  67.1 us
    reduce_scatter x1, waiting for transfers between devices, per_device(): lax.psum_scatter(lax.fori_loop(0, piece_count, add_piece, jnp.zeros((pola...  32 us
    ppermute x7, waiting for transfers between devices, shifted(): return lax.ppermute(block, axis, route)  29.6 us
    all_to_all x1, waiting for transfers between devices, per_device(): lax.all_to_all(half_occ, 'ao', split_axis=0, concat_axis=1, tiled=True)  26.5 us
    all_gather x1, local copies, waits for them, and re-layouts, per_device(): all_tensor = lax.all_gather(tensor_eff, 'ri', axis=0, tiled=True)  13.8 us
    dot_general x2, matrix products, add_piece(): jnp.einsum('qln,lnp->qp', virt_part, occ_part, preferred_element_type=jnp...  11.8 us
    unnamed x17, local copies, waits for them, and re-layouts  6.7 us
    while x15, local copies, waits for them, and re-layouts  4.9 us
  transfers between devices with their start and end apart: 10, of which 10 were waited for; matrix products, arithmetic and copies ran while one was open for 5% of the time, Pallas kernels for 0%

commit v1 on v0

--- a/solution.py
+++ b/solution.py
@@ -79,7 +79,30 @@
         )
         return product.astype(jnp.bfloat16).reshape(source_rows.shape[0], own_width, span_cols)
 
-    all_tensor = lax.all_gather(tensor_eff, "ri", axis=0, tiled=True)
+    mid_arr = lax.psum(1, "ri")
+    w2 = lax.axis_index("ri")
+    current_block, z_new, e_next = (mid_arr, w2, tensor_eff.shape[0])
+    trail = tuple(((d, (d + 1) % current_block) for d in range(current_block)))
+    all_tensor = jnp.zeros(
+        (*tensor_eff.shape[:0], current_block * e_next, *tensor_eff.shape[0 + 1 :]),
+        tensor_eff.dtype,
+    )
+    views = tuple(((d, (d - 1) % current_block) for d in range(current_block)))
+    all_tensor = lax.dynamic_update_slice_in_dim(all_tensor, tensor_eff, z_new * e_next, axis=0)
+    front = plain = tensor_eff
+    p = 1
+    t_next = current_block // 2
+    while p < t_next + 1:
+        front = lax.ppermute(front, "ri", trail)
+        all_tensor = lax.dynamic_update_slice_in_dim(
+            all_tensor, front, (z_new - p) % current_block * e_next, axis=0
+        )
+        if p < current_block - t_next:
+            plain = lax.ppermute(plain, "ri", views)
+            all_tensor = lax.dynamic_update_slice_in_dim(
+                all_tensor, plain, (z_new + p) % current_block * e_next, axis=0
+            )
+        p += 1
     kept_rows = all_tensor.shape[0] // cycle_size
     source_rows = all_tensor
     polar_source_rows = source_rows.reshape(kept_rows * lax.axis_size("ao"), own_blocks, BS, KS, BS)

time: 229 us -> 213 us (0.930)
  waiting for transfers between devices: 155 us -> 120 us
  local copies, waits for them, and re-layouts: 31.3 us -> 45 us
  starting transfers between devices: 4.5 us -> 9.16 us
    all_gather x1 -> x0, waiting for transfers between devices: 67.1 us -> none  [per_device(): all_tensor = lax.all_gather(tensor_eff, 'ri', axis=0, tiled=True)]
    ppermute x0 -> x3, waiting for transfers between devices: none -> 41.9 us  [the longest x2 35.9 us: per_device(): front = lax.ppermute(front, 'ri', trail)]
    all_gather x1 -> x0, local copies, waits for them, and re-layouts: 13.8 us -> none  [per_device(): all_tensor = lax.all_gather(tensor_eff, 'ri', axis=0, tiled=True)]
    ppermute x0 -> x3, local copies, waits for them, and re-layouts: none -> 13.7 us  [the longest x2 9.14 us: per_device(): front = lax.ppermute(front, 'ri', trail)]
    all_to_all x1, waiting for transfers between devices: 26.5 us -> 16.1 us  [per_device(): lax.all_to_all(half_occ, 'ao', split_axis=0, concat_axis=1, tiled=True)]
    dynamic_update_slice x0 -> x4, local copies, waits for them, and re-layouts: none -> 9.75 us  [the longest x2 6.55 us: per_device(): lax.dynamic_update_slice_in_dim(all_tensor, front, (z_new - p) % current_...]
    ppermute x0 -> x3, starting transfers between devices: none -> 5.11 us  [the longest x2 3.08 us: per_device(): front = lax.ppermute(front, 'ri', trail)]
    while x15 -> x7, local copies, waits for them, and re-layouts: 4.9 us -> 0.03 us
  transfers between devices with their start and end apart: 10 -> 12, of which waited for: 10 -> 11; matrix products, arithmetic and copies ran while one was open for 5% -> 18% of each run, Pallas kernels for 0% -> 0%
where the time goes in v1:
time: 213 us; the launch traced here: 212 us
  waiting for transfers between devices  120 us (56%)
  local copies, waits for them, and re-layouts  45 us (21%)
  between operations  13.6 us (6%)
  matrix products  12.7 us (6%)
  starting transfers between devices  9.16 us (4%)
  other arithmetic  6.87 us (3%)
  loops' own time  4.38 us (2%)
    ppermute x2, waiting for transfers between devices, per_device(): front = lax.ppermute(front, 'ri', trail)  35.9 us
    reduce_scatter x1, waiting for transfers between devices, per_device(): lax.psum_scatter(lax.fori_loop(0, piece_count, add_piece, jnp.zeros((pola...  33.1 us
    ppermute x7, waiting for transfers between devices, shifted(): return lax.ppermute(block, axis, route)  29.3 us
    all_to_all x1, waiting for transfers between devices, per_device(): lax.all_to_all(half_occ, 'ao', split_axis=0, concat_axis=1, tiled=True)  16.1 us
    dot_general x2, matrix products, add_piece(): jnp.einsum('qln,lnp->qp', virt_part, occ_part, preferred_element_type=jnp...  11.8 us
    ppermute x2, local copies, waits for them, and re-layouts, per_device(): front = lax.ppermute(front, 'ri', trail)  9.14 us
    dynamic_update_slice x2, local copies, waits for them, and re-layouts, per_device(): lax.dynamic_update_slice_in_dim(all_tensor, front, (z_new - p) % current_...  6.55 us
    ppermute x1, waiting for transfers between devices, per_device(): plain = lax.ppermute(plain, 'ri', views)  5.98 us
  transfers between devices with their start and end apart: 12, of which 11 were waited for; matrix products, arithmetic and copies ran while one was open for 18% of the time, Pallas kernels for 0%

profile of v1, /device:TPU:0, one launch (start us, length us, event | category | flops | bytes accessed | tf_op | source)
XLA Modules:
  0.0 212.2 jit_solution(5514306746655585732)
XLA Ops:
  6.5 0.7 convert_element_type.41
  7.2 0.1 copy.42
  7.3 0.1 mul.105
  7.5 0.1 mul.106
  7.6 0.1 copy.29
  7.7 3.2 %broadcast_multiply_fusion.1 = bf16[128,32,256]{2,1,0:T(8,128)(2,1)} fusion(bf16[128,32,256]{2,1,0:T(8,128)(2,1)} %param.13, bf16[128,256]{1,0:T(8,128)(2,1)S(1)} %copy.29), kind=kLoop, calls=%fused_computation.23 | loop fusion | flops 1048576 | bytes 4259840 | tf_op jit(solution)/shard_map/mul | solution.py:39
  10.9 3.0 %collective-permute-start.1 = (bf16[128,32,256]{2,1,0:T(8,128)(2,1)}, bf16[128,32,256]{2,1,0:T(8,128)(2,1)}, u32[]{:S(2)}, u32[]{:S(2)}) collective-permute-start(bf16[128,32,256]{2,1,0:T(8,128)(2,1)} %broadcast_multiply_fusion.1), channel_id=1, source_target_pairs={{0,8},{8,16},{16,24},{24,0},{1,9},{9,17},{17,25},{25,1},{2,10},{10... | collective-permute-start | bytes 6291464 | tf_op jit(solution)/shard_map/ppermute | solution.py:96
  14.0 2.0 collective-permute-start.2
  16.0 3.1 %copy.34 = bf16[128,32,256]{0,2,1:T(8,128)(2,1)} copy(bf16[128,32,256]{2,1,0:T(8,128)(2,1)S(1)} %copy-done.1) | data formatting | bytes 4194304 | tf_op args[0]
  19.1 0.1 mul.99
  19.2 0.1 mul.100
  19.3 0.1 mul.93
  19.3 0.1 mul.94
  19.5 0.1 multiply_bitcast_fusion
  19.6 31.3 %while.41 = (s32[]{:T(128)}, bf16[2,32,256]{2,1,0:T(8,128)(2,1)S(1)}, f32[2,1,8,32,256]{4,3,2,1,0:T(8,128)S(1)}, s32[]{:T(128)}, s32[1,8]{1,0:T(1,128)S(1)}, /*index=5*/s32[]{:T(128)}, s32[]{:T(128)}, s32[]{:T(128)}, s32[]{:T(128)}) while((s32[]{:T(128)}, bf16[2,32,256]{2,1,0:T(8,128)(2,1)S(1)}, f32[2,1,8,32,256]{4,3,2,1,0:T(8,128)S(1)}, ...), condition=%wide.region_1.2_spmd, body=%wide.region_0.1_spmd.sunk | while | flops 278559 | bytes 1409390 | solution.py:54
  19.6 0.1 collective-permute-start
  19.7 4.2 %collective-permute-done = bf16[2,32,256]{2,1,0:T(8,128)(2,1)S(1)} collective-permute-done((bf16[2,32,256]{2,1,0:T(8,128)(2,1)S(1)}, bf16[2,32,256]{2,1,0:T(8,128)(2,1)S(1)}, u32[]{:S(2)}, u32[]{:S(2)}) %collective-permute-start) | collective-permute-done | bytes 32800 | tf_op jit(solution)/shard_map/while/body/eval_jaxpr/ppermute | solution.py:14
  23.9 0.1 bitcast_add_fusion.2
  24.1 0.1 collective-permute-start
  24.2 4.2 %collective-permute-done = bf16[2,32,256]{2,1,0:T(8,128)(2,1)S(1)} collective-permute-done((bf16[2,32,256]{2,1,0:T(8,128)(2,1)S(1)}, bf16[2,32,256]{2,1,0:T(8,128)(2,1)S(1)}, u32[]{:S(2)}, u32[]{:S(2)}) %collective-permute-start) | collective-permute-done | bytes 32800 | tf_op jit(solution)/shard_map/while/body/eval_jaxpr/ppermute | solution.py:14
  28.4 0.1 bitcast_add_fusion.2
  28.5 0.1 collective-permute-start
  28.6 4.2 %collective-permute-done = bf16[2,32,256]{2,1,0:T(8,128)(2,1)S(1)} collective-permute-done((bf16[2,32,256]{2,1,0:T(8,128)(2,1)S(1)}, bf16[2,32,256]{2,1,0:T(8,128)(2,1)S(1)}, u32[]{:S(2)}, u32[]{:S(2)}) %collective-permute-start) | collective-permute-done | bytes 32800 | tf_op jit(solution)/shard_map/while/body/eval_jaxpr/ppermute | solution.py:14
  32.8 0.1 bitcast_add_fusion.2
  33.0 0.1 collective-permute-start
  33.1 4.2 %collective-permute-done = bf16[2,32,256]{2,1,0:T(8,128)(2,1)S(1)} collective-permute-done((bf16[2,32,256]{2,1,0:T(8,128)(2,1)S(1)}, bf16[2,32,256]{2,1,0:T(8,128)(2,1)S(1)}, u32[]{:S(2)}, u32[]{:S(2)}) %collective-permute-start) | collective-permute-done | bytes 32800 | tf_op jit(solution)/shard_map/while/body/eval_jaxpr/ppermute | solution.py:14
  37.3 0.1 bitcast_add_fusion.2
  37.6 4.2 %collective-permute-done = bf16[2,32,256]{2,1,0:T(8,128)(2,1)S(1)} collective-permute-done((bf16[2,32,256]{2,1,0:T(8,128)(2,1)S(1)}, bf16[2,32,256]{2,1,0:T(8,128)(2,1)S(1)}, u32[]{:S(2)}, u32[]{:S(2)}) %collective-permute-start) | collective-permute-done | bytes 32800 | tf_op jit(solution)/shard_map/while/body/eval_jaxpr/ppermute | solution.py:14
  41.8 0.1 bitcast_add_fusion.2
  42.0 4.2 %collective-permute-done = bf16[2,32,256]{2,1,0:T(8,128)(2,1)S(1)} collective-permute-done((bf16[2,32,256]{2,1,0:T(8,128)(2,1)S(1)}, bf16[2,32,256]{2,1,0:T(8,128)(2,1)S(1)}, u32[]{:S(2)}, u32[]{:S(2)}) %collective-permute-start) | collective-permute-done | bytes 32800 | tf_op jit(solution)/shard_map/while/body/eval_jaxpr/ppermute | solution.py:14
  46.2 0.1 bitcast_add_fusion.2
  46.5 4.2 %collective-permute-done = bf16[2,32,256]{2,1,0:T(8,128)(2,1)S(1)} collective-permute-done((bf16[2,32,256]{2,1,0:T(8,128)(2,1)S(1)}, bf16[2,32,256]{2,1,0:T(8,128)(2,1)S(1)}, u32[]{:S(2)}, u32[]{:S(2)}) %collective-permute-start) | collective-permute-done | bytes 32800 | tf_op jit(solution)/shard_map/while/body/eval_jaxpr/ppermute | solution.py:14
  50.7 0.1 bitcast_add_fusion.2
  51.0 0.1 mul.113
  51.1 0.1 mul.114
  51.2 1.7 broadcast_multiply_fusion
  52.9 9.4 %while.42 = (s32[]{:T(128)}, bf16[2,128,32,128]{3,2,1,0:T(8,128)(2,1)}, s32[2]{0:T(128)S(1)}, bf16[1,8,32,2,128]{4,2,1,3,0:T(8,128)(2,1)S(1)}, bf16[128,1,32,8,3...) while((s32[]{:T(128)}, bf16[2,128,32,128]{3,2,1,0:T(8,128)(2,1)}, s32[2]{0:T(128)S(1)}, ...), condition=%wide.region_3.4_spmd, body=%wide.region_2.3_spmd.sunk | while | flops 268959744 | bytes 5309063 | solution.py:70
  52.9 0.6 dynamic_slice.40
  55.5 0.5 fusion.52
  55.9 1.7 copy_dynamic-update-slice_fusion.2
  57.6 0.6 dynamic_slice.40
  60.2 0.5 fusion.52
  60.6 1.6 copy_dynamic-update-slice_fusion.2
  62.3 3.6 %all-to-all-start = ((bf16[256,32,128]{2,1,0:T(8,128)(2,1)}), bf16[256,32,128]{2,1,0:T(8,128)(2,1)S(1)}, u32[]{:S(2)}, u32[]{:S(2)}) async-start(bf16[256,32,128]{2,1,0:T(8,128)(2,1)} %bitcast.23), calls=%async_computation | async-start | bytes 4194304 | tf_op jit(solution)/shard_map/all_to_all | solution.py:73
  65.9 0.1 collective-permute-start.3
  66.0 4.5 %copy.30 = bf16[128,32,256]{0,2,1:T(8,128)(2,1)} copy(bf16[128,32,256]{2,1,0:T(8,128)(2,1)} %broadcast_multiply_fusion.1) | data formatting | bytes 4194304 | tf_op jit(solution)/shard_map/mul | solution.py:39
  70.6 4.2 %broadcast_in_dim.21 = bf16[512,32,256]{0,2,1:T(8,128)(2,1)} broadcast(bf16[]{:T(256)} %constant.121.clone.1), dimensions={} | broadcast | bytes 8388610 | tf_op jit(solution)/shard_map/broadcast_in_dim | solution.py:86
  74.8 1.6 constant_dynamic-update-slice_fusion.3
  76.4 16.1 %all-to-all-done = bf16[256,32,128]{2,1,0:T(8,128)(2,1)S(1)} async-done(((bf16[256,32,128]{2,1,0:T(8,128)(2,1)}), bf16[256,32,128]{2,1,0:T(8,128)(2,1)S(1)}, u32[]{:S(2)}, u32[]{:S(2)}) %all-to-all-start) | async-done | bytes 2097184 | tf_op jit(solution)/shard_map/all_to_all | solution.py:73
  92.5 1.3 copy-done.2
  93.8 2.2 %copy.38 = bf16[32,8,32,128]{3,2,1,0:T(8,128)(2,1)S(1)} copy(bf16[32,8,32,128]{3,2,0,1:T(8,128)(2,1)} %bitcast.129) | data formatting | bytes 4194304 | tf_op jit(solution)/shard_map/all_to_all | solution.py:73
  96.0 4.5 %copy.31 = bf16[128,32,256]{0,2,1:T(8,128)(2,1)} copy(bf16[128,32,256]{2,1,0:T(8,128)(2,1)} %collective-permute-done.1) | data formatting | bytes 4194304 | tf_op jit(solution)/shard_map/ppermute | solution.py:96
  100.5 6.0 %collective-permute-done.2 = bf16[128,32,256]{2,1,0:T(8,128)(2,1)} collective-permute-done((bf16[128,32,256]{2,1,0:T(8,128)(2,1)}, bf16[128,32,256]{2,1,0:T(8,128)(2,1)}, u32[]{:S(2)}, u32[]{:S(2)}) %collective-permute-start.2) | collective-permute-done | bytes 2097184 | tf_op jit(solution)/shard_map/ppermute | solution.py:101
  106.5 4.6 %copy.32 = bf16[128,32,256]{0,2,1:T(8,128)(2,1)} copy(bf16[128,32,256]{2,1,0:T(8,128)(2,1)} %collective-permute-done.2) | data formatting | bytes 4194304 | tf_op jit(solution)/shard_map/ppermute | solution.py:101
  111.1 3.3 %constant_dynamic-update-slice_fusion.2 = bf16[512,32,256]{0,2,1:T(8,128)(2,1)} fusion(bf16[512,32,256]{0,2,1:T(8,128)(2,1)} %constant_dynamic-update-slice_fusion.3, bf16[128,32,256]{0,2,1:T(8,128)(2,1)} %copy.31, s32[]{:T(128)S(6)} %select_n.58), kind=kLoop, calls=%fused_computation.32 | loop fusion | bytes 4194308 | tf_op jit(solution)/shard_map/dynamic_update_slice | solution.py:97
  114.4 1.6 constant_dynamic-update-slice_fusion.1
  116.0 35.9 %collective-permute-done.3 = bf16[128,32,256]{2,1,0:T(8,128)(2,1)} collective-permute-done((bf16[128,32,256]{2,1,0:T(8,128)(2,1)}, bf16[128,32,256]{2,1,0:T(8,128)(2,1)}, u32[]{:S(2)}, u32[]{:S(2)}) %collective-permute-start.3) | collective-permute-done | bytes 2097184 | tf_op jit(solution)/shard_map/ppermute | solution.py:96
  151.9 4.6 %copy.33 = bf16[128,32,256]{0,2,1:T(8,128)(2,1)} copy(bf16[128,32,256]{2,1,0:T(8,128)(2,1)} %collective-permute-done.3) | data formatting | bytes 4194304 | tf_op jit(solution)/shard_map/ppermute | solution.py:96
  156.5 3.2 %constant_dynamic-update-slice_fusion = bf16[512,32,256]{0,2,1:T(8,128)(2,1)} fusion(bf16[512,32,256]{0,2,1:T(8,128)(2,1)} %constant_dynamic-update-slice_fusion.1, bf16[128,32,256]{0,2,1:T(8,128)(2,1)} %copy.33, s32[]{:T(128)S(6)} %select_n.62), kind=kLoop, calls=%fused_computation.30 | loop fusion | bytes 4194308 | tf_op jit(solution)/shard_map/dynamic_update_slice | solution.py:97
  159.7 11.8 %while.43 = (s32[]{:T(128)}, f32[512,128]{1,0:T(8,128)S(1)}, bf16[1,8,32,256]{3,2,1,0:T(8,128)(2,1)S(1)}, bf16[512,1,32,8,32]{0,4,3,2,1:T(8,128)(2,1)}, bf16[32,...) while((s32[]{:T(128)}, f32[512,128]{1,0:T(8,128)S(1)}, ...), condition=%wide.region_5.6_spmd.clone, body=%wide.region_4.5_spmd.clone.sunk | while | flops 1612840960 | bytes 10028692 | solution.py:118
  159.7 5.9 %fusion.57 = f32[512,128]{1,0:T(8,128)S(1)} fusion(bf16[512,1,32,8,32]{0,4,3,2,1:T(8,128)(2,1)} %get-tuple-element.496, bf16[32,256,128]{2,1,0:T(8,128)(2,1)S(1)} %get-tuple-element.497, s32[]{:T(128)S(6)} %select_n.69, f32[512,128]{1,0:T(8,128)S(1)} %get-tuple-element.485, pred[]{:T(512)S(6)} %compare.7, ...), kind=kOutput, calls=%fused_computation.17.clone.1 | convolution fusion | flops 1612840960 | bytes 10028544 | tf_op jit(solution)/shard_map/while/body/eval_jaxpr/qln,lnp->qp/dot_general | solution.py:113
  165.6 5.9 %fusion.57 = f32[512,128]{1,0:T(8,128)S(1)} fusion(bf16[512,1,32,8,32]{0,4,3,2,1:T(8,128)(2,1)} %get-tuple-element.496, bf16[32,256,128]{2,1,0:T(8,128)(2,1)S(1)} %get-tuple-element.497, s32[]{:T(128)S(6)} %select_n.69, f32[512,128]{1,0:T(8,128)S(1)} %get-tuple-element.485, pred[]{:T(512)S(6)} %compare.7, ...), kind=kOutput, calls=%fused_computation.17.clone.1 | convolution fusion | flops 1612840960 | bytes 10028544 | tf_op jit(solution)/shard_map/while/body/eval_jaxpr/qln,lnp->qp/dot_general | solution.py:113
  171.5 0.7 copy-done
  172.2 33.1 %reduce-scatter.2.cloned.1.call-done = f32[64,128]{1,0:T(8,128)} async-done(((f32[512,128]{1,0:T(8,128)}), f32[64,128]{1,0:T(8,128)}) %reduce-scatter.2.cloned.1.call-update) | async-done | bytes 32784 | tf_op jit(solution)/shard_map/reduce_scatter | solution.py:117
  (57 shorter events, 0.5 us)
Async XLA Ops:
  7.7 8.3 %copy-start.1 = (bf16[128,32,256]{2,1,0:T(8,128)(2,1)S(1)}, bf16[128,32,256]{2,1,0:T(8,128)(2,1)}, u32[]{:S(2)}) copy-start(bf16[128,32,256]{2,1,0:T(8,128)(2,1)} %param.13) | copy-start | bytes 6291460
  10.9 55.0 %collective-permute-start.1 = (bf16[128,32,256]{2,1,0:T(8,128)(2,1)}, bf16[128,32,256]{2,1,0:T(8,128)(2,1)}, u32[]{:S(2)}, u32[]{:S(2)}) collective-permute-start(bf16[128,32,256]{2,1,0:T(8,128)(2,1)} %broadcast_multiply_fusion.1), channel_id=1, source_target_pairs={{0,8},{8,16},{16,24},{24,0},{1,9},{9,17},{17,25},{25,1},{2,10},{10... | collective-permute-start | bytes 6291464 | tf_op jit(solution)/shard_map/ppermute | solution.py:96
  14.0 92.6 %collective-permute-start.2 = (bf16[128,32,256]{2,1,0:T(8,128)(2,1)}, bf16[128,32,256]{2,1,0:T(8,128)(2,1)}, u32[]{:S(2)}, u32[]{:S(2)}) collective-permute-start(bf16[128,32,256]{2,1,0:T(8,128)(2,1)} %broadcast_multiply_fusion.1), channel_id=1, source_target_pairs={{0,24},{8,0},{16,8},{24,16},{1,25},{9,1},{17,9},{25,17},{2,26},{10... | collective-permute-start | bytes 6291464 | tf_op jit(solution)/shard_map/ppermute | solution.py:101
  16.0 3.1 %copy-start.7 = (s32[1,8]{1,0:T(1,128)S(1)}, s32[1,8]{1,0:T(1,128)}, u32[]{:S(2)}) copy-start(s32[1,8]{1,0:T(1,128)} %param.18) | copy-start | bytes 100
  16.0 3.3 %copy-start.8 = (s32[1,8]{1,0:T(1,128)S(1)}, s32[1,8]{1,0:T(1,128)}, u32[]{:S(2)}) copy-start(s32[1,8]{1,0:T(1,128)} %param.17) | copy-start | bytes 100
  16.0 3.4 %copy-start.5 = (bf16[32,256]{1,0:T(8,128)(2,1)S(1)}, bf16[32,256]{1,0:T(8,128)(2,1)}, u32[]{:S(2)}) copy-start(bf16[32,256]{1,0:T(8,128)(2,1)} %param.16) | copy-start | bytes 49156
  16.0 3.4 %copy-start.6 = (bf16[32,256]{1,0:T(8,128)(2,1)S(1)}, bf16[32,256]{1,0:T(8,128)(2,1)}, u32[]{:S(2)}) copy-start(bf16[32,256]{1,0:T(8,128)(2,1)} %param.15) | copy-start | bytes 49156
  16.0 3.5 %copy-start.9 = (s32[1,8]{1,0:T(1,128)S(1)}, s32[1,8]{1,0:T(1,128)}, u32[]{:S(2)}) copy-start(s32[1,8]{1,0:T(1,128)} %param.19) | copy-start | bytes 100
  19.6 4.3 %collective-permute-start = (bf16[2,32,256]{2,1,0:T(8,128)(2,1)S(1)}, bf16[2,32,256]{2,1,0:T(8,128)(2,1)S(1)}, u32[]{:S(2)}, u32[]{:S(2)}) collective-permute-start(bf16[2,32,256]{2,1,0:T(8,128)(2,1)S(1)} %get-tuple-element.434), channel_id=1, source_target_pairs={{7,0},{0,1},{1,2},{2,3},{3,4},{4,5},{5,6},{6,7},{15,8},{8,9},{9,10... | collective-permute-start | bytes 98312 | tf_op jit(solution)/shard_map/while/body/eval_jaxpr/ppermute | solution.py:14
  24.1 4.3 %collective-permute-start = (bf16[2,32,256]{2,1,0:T(8,128)(2,1)S(1)}, bf16[2,32,256]{2,1,0:T(8,128)(2,1)S(1)}, u32[]{:S(2)}, u32[]{:S(2)}) collective-permute-start(bf16[2,32,256]{2,1,0:T(8,128)(2,1)S(1)} %get-tuple-element.434), channel_id=1, source_target_pairs={{7,0},{0,1},{1,2},{2,3},{3,4},{4,5},{5,6},{6,7},{15,8},{8,9},{9,10... | collective-permute-start | bytes 98312 | tf_op jit(solution)/shard_map/while/body/eval_jaxpr/ppermute | solution.py:14
  28.5 4.3 %collective-permute-start = (bf16[2,32,256]{2,1,0:T(8,128)(2,1)S(1)}, bf16[2,32,256]{2,1,0:T(8,128)(2,1)S(1)}, u32[]{:S(2)}, u32[]{:S(2)}) collective-permute-start(bf16[2,32,256]{2,1,0:T(8,128)(2,1)S(1)} %get-tuple-element.434), channel_id=1, source_target_pairs={{7,0},{0,1},{1,2},{2,3},{3,4},{4,5},{5,6},{6,7},{15,8},{8,9},{9,10... | collective-permute-start | bytes 98312 | tf_op jit(solution)/shard_map/while/body/eval_jaxpr/ppermute | solution.py:14
  33.0 4.3 %collective-permute-start = (bf16[2,32,256]{2,1,0:T(8,128)(2,1)S(1)}, bf16[2,32,256]{2,1,0:T(8,128)(2,1)S(1)}, u32[]{:S(2)}, u32[]{:S(2)}) collective-permute-start(bf16[2,32,256]{2,1,0:T(8,128)(2,1)S(1)} %get-tuple-element.434), channel_id=1, source_target_pairs={{7,0},{0,1},{1,2},{2,3},{3,4},{4,5},{5,6},{6,7},{15,8},{8,9},{9,10... | collective-permute-start | bytes 98312 | tf_op jit(solution)/shard_map/while/body/eval_jaxpr/ppermute | solution.py:14
  37.5 4.3 %collective-permute-start = (bf16[2,32,256]{2,1,0:T(8,128)(2,1)S(1)}, bf16[2,32,256]{2,1,0:T(8,128)(2,1)S(1)}, u32[]{:S(2)}, u32[]{:S(2)}) collective-permute-start(bf16[2,32,256]{2,1,0:T(8,128)(2,1)S(1)} %get-tuple-element.434), channel_id=1, source_target_pairs={{7,0},{0,1},{1,2},{2,3},{3,4},{4,5},{5,6},{6,7},{15,8},{8,9},{9,10... | collective-permute-start | bytes 98312 | tf_op jit(solution)/shard_map/while/body/eval_jaxpr/ppermute | solution.py:14
  41.9 4.3 %collective-permute-start = (bf16[2,32,256]{2,1,0:T(8,128)(2,1)S(1)}, bf16[2,32,256]{2,1,0:T(8,128)(2,1)S(1)}, u32[]{:S(2)}, u32[]{:S(2)}) collective-permute-start(bf16[2,32,256]{2,1,0:T(8,128)(2,1)S(1)} %get-tuple-element.434), channel_id=1, source_target_pairs={{7,0},{0,1},{1,2},{2,3},{3,4},{4,5},{5,6},{6,7},{15,8},{8,9},{9,10... | collective-permute-start | bytes 98312 | tf_op jit(solution)/shard_map/while/body/eval_jaxpr/ppermute | solution.py:14
  46.4 4.3 %collective-permute-start = (bf16[2,32,256]{2,1,0:T(8,128)(2,1)S(1)}, bf16[2,32,256]{2,1,0:T(8,128)(2,1)S(1)}, u32[]{:S(2)}, u32[]{:S(2)}) collective-permute-start(bf16[2,32,256]{2,1,0:T(8,128)(2,1)S(1)} %get-tuple-element.434), channel_id=1, source_target_pairs={{7,0},{0,1},{1,2},{2,3},{3,4},{4,5},{5,6},{6,7},{15,8},{8,9},{9,10... | collective-permute-start | bytes 98312 | tf_op jit(solution)/shard_map/while/body/eval_jaxpr/ppermute | solution.py:14
  62.3 30.2 %all-to-all-start = ((bf16[256,32,128]{2,1,0:T(8,128)(2,1)}), bf16[256,32,128]{2,1,0:T(8,128)(2,1)S(1)}, u32[]{:S(2)}, u32[]{:S(2)}) async-start(bf16[256,32,128]{2,1,0:T(8,128)(2,1)} %bitcast.23), calls=%async_computation | async-start | bytes 4194304 | tf_op jit(solution)/shard_map/all_to_all | solution.py:73
  65.9 139.5 %reduce-scatter.2.cloned.1.call-start = ((), (), s32[]{:S(2)}) async-start(), calls=%async_computation.2 | async-start | bytes 294912 | tf_op jit(solution)/shard_map/reduce_scatter | solution.py:117
  65.9 85.9 %collective-permute-start.3 = (bf16[128,32,256]{2,1,0:T(8,128)(2,1)}, bf16[128,32,256]{2,1,0:T(8,128)(2,1)}, u32[]{:S(2)}, u32[]{:S(2)}) collective-permute-start(bf16[128,32,256]{2,1,0:T(8,128)(2,1)} %collective-permute-done.1), channel_id=1, source_target_pairs={{0,8},{8,16},{16,24},{24,0},{1,9},{9,17},{17,25},{25,1},{2,10},{10... | collective-permute-start | bytes 6291464 | tf_op jit(solution)/shard_map/ppermute | solution.py:96
  70.6 4.2 %copy-start.3 = (bf16[128,32,256]{0,2,1:T(8,128)(2,1)S(1)}, bf16[128,32,256]{0,2,1:T(8,128)(2,1)}, u32[]{:S(2)}) copy-start(bf16[128,32,256]{0,2,1:T(8,128)(2,1)} %copy.30) | copy-start | bytes 6291460
  92.5 1.3 copy-start.2
  111.1 3.3 %copy-start.4 = (bf16[128,32,256]{0,2,1:T(8,128)(2,1)S(1)}, bf16[128,32,256]{0,2,1:T(8,128)(2,1)}, u32[]{:S(2)}) copy-start(bf16[128,32,256]{0,2,1:T(8,128)(2,1)} %copy.32) | copy-start | bytes 6291460
  171.5 0.7 copy-start
Sparse Core Ops, SparseCore 0:
  172.3 32.9 reduce-scatter.1
